TPU v7x, 128 devices: a whole 4x4x4 slice. The times are simulated.
128 devices in a mesh: dp: 4 (over x), tensor: 32 (over z, y, core).
Axes of the slice: x: 4, y: 4, z: 4, core: 2. Of those that a mesh axis runs over, the one named last changes fastest.
Arguments:
- inputs: bfloat16 [1024, 28672], P('dp', 'tensor'), may hold values from -0.1875 to 0.1875
- output_gradient: bfloat16 [1024, 8192], P('dp', 'tensor'), may hold values from -6 to 6
- frozen: bfloat16 [8192, 28672], P('dp', 'tensor'), may hold values from -0.5905695 to 0.5905695
- adapter_down_factor: bfloat16 [64, 28672], P(None, 'tensor'), may hold values from -0.03125 to 0.03125
- adapter_up_factor: bfloat16 [8192, 64], P('dp'), may hold values from -0.3125 to 0.3125
- magnitude: float32 [8192], P('dp'), may hold values from 0.5 to 2
Outputs:
- input_gradient_rows: bfloat16 [1024, 28672], P('dp', 'tensor')
- adapter_down_gradient: float32 [64, 28672], P(None, 'tensor')
- adapter_up_gradient: float32 [8192, 64], P('dp')
- magnitude_gradient: float32 [8192], P('dp')
All inputs are finite; a program needn't handle non-finite values.
Results may differ from a plain program's by a relative error of at most 0.0057.
Values may be sent and summed in bfloat16 or wider, within the bound.
No kernel may reach another device: no remote copies, remote signals or barrier semaphores. Data moves between devices by JAX's collectives and lax.ppermute only.
A program may use at most 128 MiB of HBM per device.

v0:
```python
import jax
import jax.numpy as jnp
from jax import lax
from jax.sharding import PartitionSpec as P

adapter_scale = 2.0
epsilon = 1e-06


def local(inputs, output_gradient, frozen, adapter_down_factor, adapter_up_factor, magnitude):
    full_grad = lax.all_gather(output_gradient, "tensor", axis=1, tiled=True)
    row_grad = lax.all_to_all(full_grad, "dp", split_axis=1, concat_axis=0, tiled=True)
    combined_weight = frozen.astype(jnp.float32) + adapter_scale * jnp.dot(
        adapter_up_factor, adapter_down_factor, preferred_element_type=jnp.float32
    )
    merged_b = combined_weight.astype(jnp.bfloat16)
    squares = jnp.sum(combined_weight * combined_weight, axis=1)
    total_squares = lax.psum(squares, "tensor")
    weight_row_norm = jnp.sqrt(total_squares + epsilon)
    col_scale = magnitude / weight_row_norm
    scaled_rows = (row_grad.astype(jnp.float32) * col_scale[None, :]).astype(jnp.bfloat16)
    summed = lax.psum_scatter(
        jnp.dot(scaled_rows, merged_b, preferred_element_type=jnp.float32),
        "dp",
        scatter_dimension=0,
        tiled=True,
    )
    input_gradient_rows = summed.astype(jnp.bfloat16)
    product = lax.dot_general(
        row_grad,
        lax.all_gather(inputs, "dp", axis=0, tiled=True),
        (((0,), (0,)), ((), ())),
        preferred_element_type=jnp.float32,
    )
    gradient_row_sums = lax.psum(jnp.sum(product * combined_weight, axis=1), "tensor")
    combined_weight_gradient = col_scale[:, None] * product
    down_partial_sum = adapter_scale * lax.dot_general(
        adapter_up_factor.astype(jnp.float32),
        combined_weight_gradient,
        (((0,), (0,)), ((), ())),
        precision=lax.Precision.HIGHEST,
    )
    adapter_down_gradient = lax.psum(down_partial_sum, "dp")
    up_partial_sum = adapter_scale * jnp.dot(
        combined_weight_gradient,
        adapter_down_factor.astype(jnp.float32).T,
        precision=lax.Precision.HIGHEST,
    )
    adapter_up_gradient = lax.psum(up_partial_sum, "tensor")
    magnitude_gradient = gradient_row_sums / weight_row_norm
    return (input_gradient_rows, adapter_down_gradient, adapter_up_gradient, magnitude_gradient)


def solution(mesh):
    placed = (
        P("dp", "tensor"),
        P("dp", "tensor"),
        P("dp", "tensor"),
        P(None, "tensor"),
        P("dp", None),
        P("dp"),
    )
    return jax.shard_map(
        local,
        mesh=mesh,
        in_specs=placed,
        out_specs=(P("dp", "tensor"), P(None, "tensor"), P("dp", None), P("dp")),
        check_vma=False,
    )
```

profile of v0, /device:TPU:0, one launch (start us, length us, event | category | flops | bytes accessed | tf_op | source)
XLA Modules:
  0.0 485.6 jit_solution(599287304383377299)
XLA Ops:
  8.0 0.0 copy-start
  8.0 0.0 all-gather.3.cloned.1.call-start
  8.1 1.7 copy.12
  9.8 0.0 all-gather.3.cloned.1.call-update
  9.8 50.6 %all-gather.3.cloned.1.call-done = bf16[256,8192]{0,1:T(8,128)(2,1)} async-done(((bf16[256,256]{0,1:T(8,128)(2,1)}), bf16[256,8192]{0,1:T(8,128)(2,1)}) %all-gather.3.cloned.1.call-update) | async-done | bytes 4194320 | tf_op jit(solution)/shard_map/all_gather | solution.py:11
  60.4 0.0 copy-start.1
  60.4 5.0 %all-to-all-start = ((bf16[256,4,2048]{0,2,1:T(8,128)(2,1)}), bf16[256,4,2048]{0,2,1:T(8,128)(2,1)}, u32[]{:S(2)}, u32[]{:S(2)}) async-start(bf16[256,4,2048]{0,2,1:T(8,128)(2,1)} %bitcast.11), calls=%async_computation | async-start | bytes 8388608 | tf_op jit(solution)/shard_map/all_to_all | solution.py:12
  65.4 0.0 all-gather.5.cloned.1.call-start
  65.4 0.5 all-gather.5.cloned.1.call-update
  66.0 0.0 reduce-scatter.2.cloned.1.call-start
  66.0 6.2 %copy.14 = bf16[2048,896]{0,1:T(8,128)(2,1)} copy(bf16[2048,896]{1,0:T(8,128)(2,1)} %param.8) | data formatting | bytes 7340032 | tf_op args[2]
  72.2 0.0 copy-done
  72.2 0.0 copy-done.1
  72.2 6.1 %multiply_add_fusion = f32[2048,896]{0,1:T(8,128)} fusion(bf16[2048,896]{0,1:T(8,128)(2,1)} %copy.14, bf16[2048,64]{0,1:T(8,128)(2,1)S(1)} %copy-done, bf16[64,896]{1,0:T(8,128)(2,1)S(1)} %copy-done.1), kind=kOutput, calls=%fused_computation.3 | convolution fusion | flops 240386048 | bytes 11386880 | tf_op jit(solution)/shard_map/dot_general | solution.py:13
  78.3 51.4 %all-to-all-done = bf16[256,4,2048]{0,2,1:T(8,128)(2,1)} async-done(((bf16[256,4,2048]{0,2,1:T(8,128)(2,1)}), bf16[256,4,2048]{0,2,1:T(8,128)(2,1)}, u32[]{:S(2)}, u32[]{:S(2)}) %all-to-all-start) | async-done | bytes 4194336 | tf_op jit(solution)/shard_map/all_to_all | solution.py:12
  129.7 6.3 %copy.13 = bf16[4,256,2048]{2,1,0:T(8,128)(2,1)} copy(bf16[4,256,2048]{1,2,0:T(8,128)(2,1)} %bitcast.1) | data formatting | bytes 8388608 | tf_op jit(solution)/shard_map/all_to_all | solution.py:12
  136.0 0.0 all-gather.5.cloned.1.call-done
  136.0 0.0 copy-start.2
  136.0 12.5 %multiply_reduce_fusion = (f32[2048]{0:T(1024)S(1)}, f32[2048]{0:T(1024)S(1)}, f32[2048,896]{0,1:T(8,128)}) fusion(f32[2048,896]{0,1:T(8,128)} %multiply_add_fusion, bf16[1024,2048]{1,0:T(8,128)(2,1)} %bitcast.12, bf16[1024,896]{1,0:T(8,128)(2,1)} %all-gather.5.cloned.1.call-done), kind=kOutput, calls=%fused_computation.1 | convolution fusion | flops 3765432320 | bytes 20725760 | tf_op jit(solution)/shard_map/dot_general | solution.py:29
  148.5 125.4 %all-reduce = (f32[2048]{0:T(1024)S(1)}, f32[2048]{0:T(1024)S(1)}) all-reduce(f32[2048]{0:T(1024)S(1)} %get-tuple-element.5, f32[2048]{0:T(1024)S(1)} %get-tuple-element.4), channel_id=1, replica_groups=mesh['dp'=4,'tensor'=32] {'tensor'}, use_global_device_ids=true, to_apply=%region_1.0 | all-reduce | flops 4096 | bytes 32768 | tf_op jit(solution)/shard_map/psum | solution.py:18
  273.9 0.0 copy-done.2
  273.9 0.6 fusion.18
  274.5 10.7 %fusion.4 = f32[1024,896]{1,0:T(8,128)} fusion(bf16[1024,2048]{1,0:T(8,128)(2,1)} %bitcast.13, f32[2048]{0:T(1024)S(1)} %get-tuple-element.9, f32[2048,896]{0,1:T(8,128)} %multiply_add_fusion), kind=kOutput, calls=%fused_computation.8 | convolution fusion | flops 3766222848 | bytes 15212544 | tf_op jit(solution)/shard_map/dot_general | solution.py:23
  285.2 0.0 reduce-scatter.2.cloned.1.call-update
  285.2 0.2 all-reduce.4.cloned.1.call-start
  285.5 7.9 %fusion.15 = f32[64,896]{1,0:T(8,128)} fusion(bf16[2048,64]{0,1:T(8,128)(2,1)S(1)} %copy-done, f32[2048,896]{0,1:T(8,128)} %get-tuple-element.10, f32[2048]{0:T(1024)S(1)} %get-tuple-element.9), kind=kOutput, calls=%fused_computation.15 | convolution fusion | flops 1411178496 | bytes 7839744 | tf_op jit(solution)/shard_map/dot_general | solution.py:37
  293.3 0.0 all-reduce.4.cloned.1.call-update
  293.4 0.0 all-reduce.6.cloned.1.call-start
  293.4 7.0 %fusion.9 = f32[2048,64]{0,1:T(8,128)} fusion(bf16[64,896]{1,0:T(8,128)(2,1)S(1)} %copy-done.1, f32[2048,896]{0,1:T(8,128)} %get-tuple-element.10, f32[2048]{0:T(1024)S(1)} %get-tuple-element.9), kind=kOutput, calls=%fused_computation.13 | convolution fusion | flops 1411252224 | bytes 7987200 | tf_op jit(solution)/shard_map/dot_general | solution.py:44
  300.4 0.0 all-reduce.6.cloned.1.call-update
  300.5 21.8 %reduce-scatter.2.cloned.1.call-done = f32[256,896]{1,0:T(8,128)} async-done(((f32[1024,896]{1,0:T(8,128)}), f32[256,896]{1,0:T(8,128)}) %reduce-scatter.2.cloned.1.call-update) | async-done | bytes 917520 | tf_op jit(solution)/shard_map/reduce_scatter | solution.py:22
  322.2 2.0 convert_element_type.21
  324.2 42.0 %all-reduce.4.cloned.1.call-done = f32[64,896]{1,0:T(8,128)} async-done(((f32[64,896]{1,0:T(8,128)}), f32[64,896]{1,0:T(8,128)}) %all-reduce.4.cloned.1.call-update) | async-done | bytes 229392 | tf_op jit(solution)/shard_map/psum | solution.py:43
  366.2 108.3 %all-reduce.6.cloned.1.call-done = f32[2048,64]{0,1:T(8,128)} async-done(((f32[2048,64]{0,1:T(8,128)}), f32[2048,64]{0,1:T(8,128)}) %all-reduce.6.cloned.1.call-update) | async-done | bytes 524304 | tf_op jit(solution)/shard_map/psum | solution.py:49
  474.5 1.6 copy.17
  476.2 1.9 copy.18
Async XLA Ops:
  8.0 64.2 %copy-start = (bf16[2048,64]{0,1:T(8,128)(2,1)S(1)}, bf16[2048,64]{0,1:T(8,128)(2,1)}, u32[]{:S(2)}) copy-start(bf16[2048,64]{0,1:T(8,128)(2,1)} %param.10) | copy-start | bytes 786436
  8.0 52.4 %all-gather.3.cloned.1.call-start = ((), (), s32[]{:S(2)}) async-start(), calls=%async_computation.2 | async-start | bytes 4325376 | tf_op jit(solution)/shard_map/all_gather | solution.py:11
  60.4 11.8 %copy-start.1 = (bf16[64,896]{1,0:T(8,128)(2,1)S(1)}, bf16[64,896]{1,0:T(8,128)(2,1)}, u32[]{:S(2)}) copy-start(bf16[64,896]{1,0:T(8,128)(2,1)} %param.9) | copy-start | bytes 344068
  60.4 69.3 %all-to-all-start = ((bf16[256,4,2048]{0,2,1:T(8,128)(2,1)}), bf16[256,4,2048]{0,2,1:T(8,128)(2,1)}, u32[]{:S(2)}, u32[]{:S(2)}) async-start(bf16[256,4,2048]{0,2,1:T(8,128)(2,1)} %bitcast.11), calls=%async_computation | async-start | bytes 8388608 | tf_op jit(solution)/shard_map/all_to_all | solution.py:12
  65.4 70.6 %all-gather.5.cloned.1.call-start = ((), (), s32[]{:S(2)}) async-start(), calls=%async_computation.4 | async-start | bytes 2293760 | tf_op jit(solution)/shard_map/all_gather | solution.py:31
  66.0 256.3 %reduce-scatter.2.cloned.1.call-start = ((), (), s32[]{:S(2)}) async-start(), calls=%async_computation.3 | async-start | bytes 4587520 | tf_op jit(solution)/shard_map/reduce_scatter | solution.py:22
  136.0 137.9 %copy-start.2 = (f32[2048]{0:T(1024)S(1)}, f32[2048]{0:T(1024)}, u32[]{:S(2)}) copy-start(f32[2048]{0:T(1024)} %param.11) | copy-start | bytes 24580
  285.2 81.0 %all-reduce.4.cloned.1.call-start = ((), (), s32[]{:S(2)}) async-start(), calls=%async_computation.5 | async-start | bytes 458752 | tf_op jit(solution)/shard_map/psum | solution.py:43
  293.4 181.2 %all-reduce.6.cloned.1.call-start = ((), (), s32[]{:S(2)}) async-start(), calls=%async_computation.6 | async-start | bytes 1048576 | tf_op jit(solution)/shard_map/psum | solution.py:49
Sparse Core Ops, SparseCore 0:
  11.7 48.6 all-gather.2
Sparse Core Ops, SparseCore 1:
  67.5 42.7 all-gather.4
  285.3 36.9 reduce-scatter.1
  325.0 41.2 all-reduce.3
  370.0 104.4 all-reduce.5
where the time goes:
time: 487 us; the launch traced here: 486 us
  waiting for transfers between devices  275 us (56%)
  blocking collectives  125 us (26%)
  matrix products  44.3 us (9%)
  local copies, waits for them, and re-layouts  17.7 us (4%)
  between operations  15.7 us (3%)
  starting transfers between devices  5.4 us (1%)
    psum x1, blocking collectives, local(): total_squares = lax.psum(squares, 'tensor')  125 us
    psum x1, waiting for transfers between devices, local(): adapter_up_gradient = lax.psum(up_partial_sum, 'tensor')  108 us
    all_to_all x1, waiting for transfers between devices, local(): lax.all_to_all(full_grad, 'dp', split_axis=1, concat_axis=0, tiled=True)  51.4 us
    all_gather x1, waiting for transfers between devices, local(): full_grad = lax.all_gather(output_gradient, 'tensor', axis=1, tiled=True)  50.6 us
    psum x1, waiting for transfers between devices, local(): adapter_down_gradient = lax.psum(down_partial_sum, 'dp')  42 us
    reduce_scatter x1, waiting for transfers between devices, local(): lax.psum_scatter(jnp.dot(scaled_rows, merged_b, preferred_element_type=jn...  21.8 us
    dot_general x1, matrix products, local(): lax.dot_general(row_grad, lax.all_gather(inputs, 'dp', axis=0, tiled=True...  12.5 us
    unnamed x10, local copies, waits for them, and re-layouts  11.4 us
  transfers between devices with their start and end apart: 6, of which 5 were waited for; matrix products, arithmetic and copies ran while one was open for 7% of the time, Pallas kernels for 0%

commit v1 on v0

v1 whole, which is shorter than its diff:
```python
import jax
import jax.numpy as jnp
from jax import lax
from jax.sharding import PartitionSpec as P

adapter_scale = 2.0
epsilon = 1e-06


def split_bf16(v):
    hi = v.astype(jnp.bfloat16)
    lo = (v - hi.astype(jnp.float32)).astype(jnp.bfloat16)
    return hi, lo


def dot2(spec, a, b_pair):
    hi, lo = b_pair
    return jnp.einsum(spec, a, hi, preferred_element_type=jnp.float32) + jnp.einsum(
        spec, a, lo, preferred_element_type=jnp.float32
    )


def transpose_pairs(n_dp, n_t):
    group = n_t // n_dp
    pairs = []
    for d in range(n_dp):
        for t in range(n_t):
            b, rest = divmod(t, group)
            pairs.append((d * n_t + t, b * n_t + d * group + rest))
    return pairs


def shift_pairs(n, k):
    return [(i, (i + k) % n) for i in range(n)]


def gather_dp(v, n_dp, d):
    out = jnp.zeros((n_dp,) + v.shape, v.dtype)
    out = lax.dynamic_update_index_in_dim(out, v, d, 0)
    for k in range(1, n_dp):
        piece = lax.ppermute(v, "dp", shift_pairs(n_dp, k))
        out = lax.dynamic_update_index_in_dim(out, piece, (d + n_dp - k) % n_dp, 0)
    return out


def reduce_scatter_dp(part, n_dp, d, axis):
    acc = lax.dynamic_index_in_dim(part, d, axis, keepdims=False)
    for k in range(1, n_dp):
        piece = lax.dynamic_index_in_dim(part, (d + k) % n_dp, axis, keepdims=False)
        piece = lax.ppermute(piece.astype(jnp.bfloat16), "dp", shift_pairs(n_dp, k))
        acc = acc + piece.astype(jnp.float32)
    return acc


def allreduce(v, axis, n):
    k = 1
    while k < n:
        v = v + lax.ppermute(v, axis, [(i, i ^ k) for i in range(n)])
        k *= 2
    return v


def make_local(n_dp, n_t):
    pairs = transpose_pairs(n_dp, n_t)

    def local(inputs, output_gradient, frozen, adapter_down_factor, adapter_up_factor, magnitude):
        d = lax.axis_index("dp")
        t = lax.axis_index("tensor")
        tok, cols = inputs.shape
        rows = frozen.shape[0]
        rank = adapter_down_factor.shape[0]

        og_p = lax.ppermute(output_gradient, ("dp", "tensor"), pairs)
        og_all = lax.all_gather(og_p, "tensor", axis=1, tiled=True).reshape(tok, n_dp, rows)
        x_all = gather_dp(inputs, n_dp, d)

        merged = frozen.astype(jnp.float32) + adapter_scale * jnp.dot(
            adapter_up_factor, adapter_down_factor, preferred_element_type=jnp.float32
        )
        merged_b = merged.astype(jnp.bfloat16)
        squares = jnp.sum(merged * merged, axis=1)
        h_local = jnp.dot(inputs, adapter_down_factor.T, preferred_element_type=jnp.float32)

        first = allreduce(jnp.concatenate([squares, h_local.reshape(-1)]), "tensor", n_t)
        total_squares = first[:rows]
        h_all = gather_dp(first[rows:].reshape(tok, rank), n_dp, d)

        weight_row_norm = jnp.sqrt(total_squares + epsilon)
        col_scale = magnitude / weight_row_norm

        scaled = (og_all.astype(jnp.float32) * col_scale).astype(jnp.bfloat16)
        ig_part = jnp.einsum("tbj,ji->bti", scaled, merged_b, preferred_element_type=jnp.float32)
        input_gradient_rows = reduce_scatter_dp(ig_part, n_dp, d, 0).astype(jnp.bfloat16)

        product = jnp.einsum("tbj,bti->ji", og_all, x_all, preferred_element_type=jnp.float32)
        grad_scale = allreduce(jnp.sum(product * merged, axis=1), "tensor", n_t)

        w = col_scale[:, None] * adapter_up_factor.astype(jnp.float32)
        g_all = allreduce(dot2("tbj,jr->btr", og_all, split_bf16(w)), "dp", n_dp)

        gh, gl = split_bf16(g_all)
        adapter_down_gradient = adapter_scale * (
            jnp.einsum("btr,bti->ri", gh, x_all, preferred_element_type=jnp.float32)
            + jnp.einsum("btr,bti->ri", gl, x_all, preferred_element_type=jnp.float32)
        )
        up = dot2("tbj,btr->jr", og_all, split_bf16(h_all))
        adapter_up_gradient = adapter_scale * (col_scale[:, None] * up)
        magnitude_gradient = grad_scale / weight_row_norm
        return (input_gradient_rows, adapter_down_gradient, adapter_up_gradient, magnitude_gradient)

    return local


def solution(mesh):
    n_dp = mesh.shape["dp"]
    n_t = mesh.shape["tensor"]
    placed = (
        P("dp", "tensor"),
        P("dp", "tensor"),
        P("dp", "tensor"),
        P(None, "tensor"),
        P("dp", None),
        P("dp"),
    )
    return jax.shard_map(
        make_local(n_dp, n_t),
        mesh=mesh,
        in_specs=placed,
        out_specs=(P("dp", "tensor"), P(None, "tensor"), P("dp", None), P("dp")),
        check_vma=False,
    )
```

time: 487 us -> 160 us (0.33)
  waiting for transfers between devices: 275 us -> 49.1 us
  blocking collectives: 125 us -> 0 us
  starting transfers between devices: 5.4 us -> 44.1 us
  matrix products: 44.3 us -> 31.1 us
    psum x2 -> x0, waiting for transfers between devices: 150 us -> none  [the longest x1 108 us: local(): adapter_up_gradient = lax.psum(up_partial_sum, 'tensor')]
    psum x1 -> x0, blocking collectives: 125 us -> none  [local(): total_squares = lax.psum(squares, 'tensor')]
    all_to_all x1 -> x0, waiting for transfers between devices: 51.4 us -> none  [local(): lax.all_to_all(full_grad, 'dp', split_axis=1, concat_axis=0, tiled=True)]
    all_gather x2 -> x1, waiting for transfers between devices: 50.6 us -> 0.02 us  [local(): lax.all_gather(og_p, 'tensor', axis=1, tiled=True).reshape(tok, n_dp, rows)]
    ppermute x0 -> x22, waiting for transfers between devices: none -> 49.1 us  [the longest x12 49.1 us: allreduce(): v = v + lax.ppermute(v, axis, [(i, i ^ k) for i in range(n)])]
    ppermute x0 -> x22, starting transfers between devices: none -> 44 us  [the longest x6 22.9 us: gather_dp(): piece = lax.ppermute(v, 'dp', shift_pairs(n_dp, k))]
    reduce_scatter x1 -> x0, waiting for transfers between devices: 21.8 us -> none  [local(): lax.psum_scatter(jnp.dot(scaled_rows, merged_b, preferred_element_type=jn...]
    dot_general x4 -> x9, matrix products: 38.1 us -> 24.7 us  [the longest x1 7.54 us: local(): jnp.einsum('tbj,bti->ji', og_all, x_all, preferred_element_type=jnp.float32)]
  transfers between devices with their start and end apart: 6 -> 23, of which waited for: 5 -> 10; matrix products, arithmetic and copies ran while one was open for 7% -> 24% of each run, Pallas kernels for 0% -> 0%
where the time goes in v1:
time: 160 us; the launch traced here: 159 us
  waiting for transfers between devices  49.1 us (31%)
  starting transfers between devices  44.1 us (28%)
  matrix products  31.1 us (19%)
  local copies, waits for them, and re-layouts  19.1 us (12%)
  between operations  14.5 us (9%)
    ppermute x12, waiting for transfers between devices, allreduce(): v = v + lax.ppermute(v, axis, [(i, i ^ k) for i in range(n)])  49.1 us
    ppermute x6, starting transfers between devices, gather_dp(): piece = lax.ppermute(v, 'dp', shift_pairs(n_dp, k))  22.9 us
    ppermute x12, starting transfers between devices, allreduce(): v = v + lax.ppermute(v, axis, [(i, i ^ k) for i in range(n)])  16.7 us
    unnamed x15, local copies, waits for them, and re-layouts  9.63 us
    dot_general x1, matrix products, local(): jnp.einsum('tbj,bti->ji', og_all, x_all, preferred_element_type=jnp.float32)  7.54 us
    dot_general x1, matrix products, local(): jnp.einsum('tbj,ji->bti', scaled, merged_b, preferred_element_type=jnp.fl...  6.53 us
    broadcast_in_dim x6, local copies, waits for them, and re-layouts, gather_dp(): out = lax.dynamic_update_index_in_dim(out, piece, (d + n_dp - k) % n_dp, 0)  6.47 us
    dot_general x1, matrix products, local(): jnp.dot(adapter_up_factor, adapter_down_factor, preferred_element_type=jn...  6.43 us
  transfers between devices with their start and end apart: 23, of which 10 were waited for; matrix products, arithmetic and copies ran while one was open for 24% of the time, Pallas kernels for 0%

profile of v1, /device:TPU:0, one launch (start us, length us, event | category | flops | bytes accessed | tf_op | source)
XLA Modules:
  0.0 158.9 jit_solution(10402095207626134916)
XLA Ops:
  7.2 0.0 all-gather.2.cloned.1.call-start
  7.2 1.0 copy.19
  8.2 0.8 collective-permute-start
  9.1 0.6 copy-done.4
  9.7 6.2 %copy.18 = bf16[2048,896]{0,1:T(8,128)(2,1)} copy(bf16[2048,896]{1,0:T(8,128)(2,1)} %param.8) | data formatting | bytes 7340032 | tf_op args[2]
  16.0 1.3 fusion.32
  17.2 0.1 reshape.30
  17.3 6.4 %multiply_reduce_fusion = (f32[2048]{0:T(1024)S(1)}, f32[2048,896]{0,1:T(8,128)}) fusion(bf16[2048,64]{0,1:T(8,128)(2,1)S(1)} %copy-done.2, bf16[64,896]{1,0:T(8,128)(2,1)S(1)} %copy-done, bf16[2048,896]{0,1:T(8,128)(2,1)} %copy.18), kind=kOutput, calls=%fused_computation.3 | convolution fusion | flops 244054016 | bytes 11395072 | tf_op jit(solution)/shard_map/dot_general | solution.py:77
  23.8 9.0 %collective-permute-start.11 = (bf16[256,896]{1,0:T(8,128)(2,1)}, bf16[256,896]{1,0:T(8,128)(2,1)}, u32[]{:S(2)}, u32[]{:S(2)}) collective-permute-start(bf16[256,896]{1,0:T(8,128)(2,1)} %param.6), channel_id=1, source_target_pairs={{0,32},{32,64},{64,96},{96,0},{1,33},{33,65},{65,97},{97,1},{2,34}... | collective-permute-start | bytes 1376264 | tf_op jit(solution)/shard_map/ppermute | solution.py:41
  32.8 8.0 %collective-permute-start.12 = (bf16[256,896]{1,0:T(8,128)(2,1)}, bf16[256,896]{1,0:T(8,128)(2,1)S(1)}, u32[]{:S(2)}, u32[]{:S(2)}) collective-permute-start(bf16[256,896]{1,0:T(8,128)(2,1)} %param.6), channel_id=1, source_target_pairs={{0,64},{32,96},{64,0},{96,32},{1,65},{33,97},{65,1},{97,33},{2,66}... | collective-permute-start | bytes 1376264 | tf_op jit(solution)/shard_map/ppermute | solution.py:41
  40.8 1.4 collective-permute-start.13
  42.2 1.7 %collective-permute-start.2 = (f32[18432]{0:T(1024)S(1)}, f32[18432]{0:T(1024)S(1)}, u32[]{:S(2)}, u32[]{:S(2)}) collective-permute-start(f32[18432]{0:T(1024)S(1)} %fusion.31), channel_id=1, source_target_pairs={{0,2},{1,3},{2,0},{3,1},{4,6},{5,7},{6,4},{7,5},{8,10},{9,11},{10,... | collective-permute-start | bytes 221192 | tf_op jit(solution)/shard_map/ppermute | solution.py:58
  43.9 2.8 %collective-permute-done.2 = f32[18432]{0:T(1024)S(1)} collective-permute-done((f32[18432]{0:T(1024)S(1)}, f32[18432]{0:T(1024)S(1)}, u32[]{:S(2)}, u32[]{:S(2)}) %collective-permute-start.2) | collective-permute-done | bytes 73760 | tf_op jit(solution)/shard_map/ppermute | solution.py:58
  46.6 3.3 %collective-permute-start.3 = (f32[18432]{0:T(1024)S(1)}, f32[18432]{0:T(1024)S(1)}, u32[]{:S(2)}, u32[]{:S(2)}) collective-permute-start(f32[18432]{0:T(1024)S(1)} %add.132), channel_id=1, source_target_pairs={{0,4},{1,5},{2,6},{3,7},{4,0},{5,1},{6,2},{7,3},{8,12},{9,13},{10,... | collective-permute-start | bytes 221192 | tf_op jit(solution)/shard_map/ppermute | solution.py:58
  49.9 2.7 %collective-permute-done.3 = f32[18432]{0:T(1024)S(1)} collective-permute-done((f32[18432]{0:T(1024)S(1)}, f32[18432]{0:T(1024)S(1)}, u32[]{:S(2)}, u32[]{:S(2)}) %collective-permute-start.3) | collective-permute-done | bytes 73760 | tf_op jit(solution)/shard_map/ppermute | solution.py:58
  52.6 0.1 collective-permute-start.4
  52.7 1.2 copy.24
  54.0 4.7 %collective-permute-done.4 = f32[18432]{0:T(1024)S(1)} collective-permute-done((f32[18432]{0:T(1024)S(1)}, f32[18432]{0:T(1024)S(1)}, u32[]{:S(2)}, u32[]{:S(2)}) %collective-permute-start.4) | collective-permute-done | bytes 73760 | tf_op jit(solution)/shard_map/ppermute | solution.py:58
  58.7 1.2 collective-permute-start.5
  59.9 0.1 broadcast_in_dim.35
  60.0 5.2 %collective-permute-done.5 = f32[18432]{0:T(1024)S(1)} collective-permute-done((f32[18432]{0:T(1024)S(1)}, f32[18432]{0:T(1024)S(1)}, u32[]{:S(2)}, u32[]{:S(2)}) %collective-permute-start.5) | collective-permute-done | bytes 73760 | tf_op jit(solution)/shard_map/ppermute | solution.py:58
  65.2 0.1 broadcast_in_dim.41
  65.3 0.1 slice.18
  65.4 1.5 collective-permute-start.14
  66.9 0.5 collective-permute-start.15
  67.3 0.1 copy.30
  67.4 2.6 %collective-permute-start.16 = (f32[256,64]{1,0:T(8,128)S(1)}, f32[256,64]{1,0:T(8,128)S(1)}, u32[]{:S(2)}, u32[]{:S(2)}) collective-permute-start(f32[256,64]{1,0:T(8,128)S(1)} %slice.18), channel_id=1, source_target_pairs={{0,96},{32,0},{64,32},{96,64},{1,97},{33,1},{65,33},{97,65},{2,98}... | collective-permute-start | bytes 196616 | tf_op jit(solution)/shard_map/ppermute | solution.py:41
  70.0 1.2 copy.25
  71.3 0.8 copy-done.3
  72.0 1.2 copy.26
  73.3 2.0 %copy.27 = bf16[1,256,896]{1,2,0:T(8,128)(2,1)} copy(bf16[1,256,896]{2,1,0:T(8,128)(2,1)} %bitcast.16) | data formatting | bytes 917504 | tf_op jit(solution)/shard_map/jit(dynamic_update_index_in_dim)/broadcast_in_dim | solution.py:42
  75.4 1.1 constant_dynamic-update-slice_fusion.4
  76.4 0.0 all-gather.2.cloned.1.call-done
  76.4 7.5 %fusion = f32[2048]{0:T(1024)S(1)} fusion(f32[2048,896]{0,1:T(8,128)} %get-tuple-element.18, bf16[4,256,896]{1,2,0:T(8,128)(2,1)S(1)} %constant_dynamic-update-slice_fusion.4, bf16[256,4,2048]{0,2,1:T(8,128)(2,1)} %bitcast.81), kind=kOutput, calls=%fused_computation.2 | convolution fusion | flops 3761764352 | bytes 13377536 | tf_op jit(solution)/shard_map/tbj,bti->ji/dot_general | solution.py:95
  84.0 0.1 collective-permute-start.17
  84.2 1.0 copy.31
  85.1 0.1 collective-permute-done.17
  85.3 1.8 %collective-permute-start.18 = (f32[2048]{0:T(1024)S(1)}, f32[2048]{0:T(1024)S(1)}, u32[]{:S(2)}, u32[]{:S(2)}) collective-permute-start(f32[2048]{0:T(1024)S(1)} %add.157), channel_id=1, source_target_pairs={{0,2},{1,3},{2,0},{3,1},{4,6},{5,7},{6,4},{7,5},{8,10},{9,11},{10,... | collective-permute-start | bytes 24584 | tf_op jit(solution)/shard_map/ppermute | solution.py:58
  87.1 1.0 copy.32
  88.1 0.8 collective-permute-done.18
  88.9 3.4 %collective-permute-start.19 = (f32[2048]{0:T(1024)S(1)}, f32[2048]{0:T(1024)S(1)}, u32[]{:S(2)}, u32[]{:S(2)}) collective-permute-start(f32[2048]{0:T(1024)S(1)} %add.158), channel_id=1, source_target_pairs={{0,4},{1,5},{2,6},{3,7},{4,0},{5,1},{6,2},{7,3},{8,12},{9,13},{10,... | collective-permute-start | bytes 24584 | tf_op jit(solution)/shard_map/ppermute | solution.py:58
  92.3 0.1 copy.33
  92.4 1.7 %collective-permute-done.19 = f32[2048]{0:T(1024)S(1)} collective-permute-done((f32[2048]{0:T(1024)S(1)}, f32[2048]{0:T(1024)S(1)}, u32[]{:S(2)}, u32[]{:S(2)}) %collective-permute-start.19) | collective-permute-done | bytes 8224 | tf_op jit(solution)/shard_map/ppermute | solution.py:58
  94.1 1.3 collective-permute-start.20
  95.4 2.4 %collective-permute-done.20 = f32[2048]{0:T(1024)S(1)} collective-permute-done((f32[2048]{0:T(1024)S(1)}, f32[2048]{0:T(1024)S(1)}, u32[]{:S(2)}, u32[]{:S(2)}) %collective-permute-start.20) | collective-permute-done | bytes 8224 | tf_op jit(solution)/shard_map/ppermute | solution.py:58
  97.7 3.2 %collective-permute-start.21 = (f32[2048]{0:T(1024)S(1)}, f32[2048]{0:T(1024)S(1)}, u32[]{:S(2)}, u32[]{:S(2)}) collective-permute-start(f32[2048]{0:T(1024)S(1)} %add.160), channel_id=1, source_target_pairs={{0,16},{1,17},{2,18},{3,19},{4,20},{5,21},{6,22},{7,23},{8,24},{9,... | collective-permute-start | bytes 24584 | tf_op jit(solution)/shard_map/ppermute | solution.py:58
  100.9 3.6 %convolution_bitcast_fusion = f32[64,2048]{1,0:T(8,128)S(1)} fusion(bf16[256,4,2048]{0,2,1:T(8,128)(2,1)} %bitcast.82, f32[4,256,64]{1,2,0:T(8,128)S(1)} %constant_dynamic-update-slice_fusion), kind=kOutput, calls=%fused_computation.9 | convolution fusion | flops 268697600 | bytes 4980736 | tf_op jit(solution)/shard_map/tbj,btr->jr/dot_general | solution.py:18
  104.5 0.6 add_divide_fusion
  105.1 0.8 fusion.22
  105.9 6.5 %fusion.1 = f32[896,256,4]{1,0,2:T(8,128)S(1)} fusion(bf16[256,4,2048]{0,2,1:T(8,128)(2,1)S(1)} %bitcast.84, f32[2048]{0:T(1024)S(1)} %get-tuple-element.16, f32[2048,896]{0,1:T(8,128)} %get-tuple-element.18), kind=kOutput, calls=%fused_computation.5 | convolution fusion | flops 3766222848 | bytes 15212544 | tf_op jit(solution)/shard_map/tbj,ji->bti/dot_general | solution.py:92
  112.5 0.1 fusion.16
  112.6 0.1 collective-permute-start.6
  112.7 1.5 collective-permute-start.7
  114.2 2.0 %collective-permute-start.8 = (bf16[256,896]{0,1:T(8,128)(2,1)S(1)}, bf16[256,896]{0,1:T(8,128)(2,1)S(1)}, u32[]{:S(2)}, u32[]{:S(2)}) collective-permute-start(bf16[256,896]{0,1:T(8,128)(2,1)S(1)} %get-tuple-element.13), channel_id=1, source_target_pairs={{0,96},{32,0},{64,32},{96,64},{1,97},{33,1},{65,33},{97,65},{2,98}... | collective-permute-start | bytes 1376264 | tf_op jit(solution)/shard_map/ppermute | solution.py:50
  116.2 0.8 fusion.9
  117.0 0.7 collective-permute-start.9
  117.7 2.2 %fusion.8 = f32[2048,64]{0,1:T(8,128)} fusion(f32[64,2048]{1,0:T(8,128)S(1)} %convolution_bitcast_fusion, bf16[256,4,2048]{0,2,1:T(8,128)(2,1)S(1)} %bitcast.86, f32[2048]{0:T(1024)S(1)} %get-tuple-element.16, f32[4,256,64]{1,2,0:T(8,128)S(1)} %constant_dynamic-update-slice_fusion), kind=kOutput, calls=%fused_computation.14 | convolution fusion | flops 268894208 | bytes 5513216 | tf_op jit(solution)/shard_map/tbj,btr->jr/dot_general | solution.py:18
  119.9 22.2 %collective-permute-done.9 = f32[4,256,64]{1,2,0:T(8,128)S(1)} collective-permute-done((f32[4,256,64]{1,2,0:T(8,128)S(1)}, f32[4,256,64]{1,2,0:T(8,128)S(1)}, u32[]{:S(2)}, u32[]{:S(2)}) %collective-permute-start.9) | collective-permute-done | bytes 262176 | tf_op jit(solution)/shard_map/ppermute | solution.py:58
  142.1 0.1 collective-permute-start.10
  142.2 0.2 fusion.14
  142.5 1.0 copy.37
  143.4 6.6 %collective-permute-done.10 = f32[4,256,64]{1,2,0:T(8,128)S(1)} collective-permute-done((f32[4,256,64]{1,2,0:T(8,128)S(1)}, f32[4,256,64]{1,2,0:T(8,128)S(1)}, u32[]{:S(2)}, u32[]{:S(2)}) %collective-permute-start.10) | collective-permute-done | bytes 262176 | tf_op jit(solution)/shard_map/ppermute | solution.py:58
  150.1 0.7 convolution_bitcast_fusion.2
  150.7 1.4 fusion.11
  (44 shorter events, 0.4 us)
Async XLA Ops:
  7.2 8.8 %copy-start = (bf16[64,896]{1,0:T(8,128)(2,1)S(1)}, bf16[64,896]{1,0:T(8,128)(2,1)}, u32[]{:S(2)}) copy-start(bf16[64,896]{1,0:T(8,128)(2,1)} %param.9) | copy-start | bytes 344068
  7.2 69.3 %all-gather.2.cloned.1.call-start = ((), (), s32[]{:S(2)}) async-start(), calls=%async_computation | async-start | bytes 4325376 | tf_op jit(solution)/shard_map/all_gather | solution.py:74
  8.2 9.1 %copy-start.2 = (bf16[2048,64]{0,1:T(8,128)(2,1)S(1)}, bf16[2048,64]{0,1:T(8,128)(2,1)}, u32[]{:S(2)}) copy-start(bf16[2048,64]{0,1:T(8,128)(2,1)} %param.10) | copy-start | bytes 786436
  8.2 0.8 collective-permute-start
  9.1 0.7 copy-start.4
  23.8 18.4 %collective-permute-start.1 = (f32[18432]{0:T(1024)S(1)}, f32[18432]{0:T(1024)S(1)}, u32[]{:S(2)}, u32[]{:S(2)}) collective-permute-start(f32[18432]{0:T(1024)S(1)} %pad_maximum_fusion), channel_id=1, source_target_pairs={{0,1},{1,0},{2,3},{3,2},{4,5},{5,4},{6,7},{7,6},{8,9},{9,8},{10,11... | collective-permute-start | bytes 221192 | tf_op jit(solution)/shard_map/ppermute | solution.py:58
  23.8 43.6 %collective-permute-start.11 = (bf16[256,896]{1,0:T(8,128)(2,1)}, bf16[256,896]{1,0:T(8,128)(2,1)}, u32[]{:S(2)}, u32[]{:S(2)}) collective-permute-start(bf16[256,896]{1,0:T(8,128)(2,1)} %param.6), channel_id=1, source_target_pairs={{0,32},{32,64},{64,96},{96,0},{1,33},{33,65},{65,97},{97,1},{2,34}... | collective-permute-start | bytes 1376264 | tf_op jit(solution)/shard_map/ppermute | solution.py:41
  32.8 38.5 %collective-permute-start.12 = (bf16[256,896]{1,0:T(8,128)(2,1)}, bf16[256,896]{1,0:T(8,128)(2,1)S(1)}, u32[]{:S(2)}, u32[]{:S(2)}) collective-permute-start(bf16[256,896]{1,0:T(8,128)(2,1)} %param.6), channel_id=1, source_target_pairs={{0,64},{32,96},{64,0},{96,32},{1,65},{33,97},{65,1},{97,33},{2,66}... | collective-permute-start | bytes 1376264 | tf_op jit(solution)/shard_map/ppermute | solution.py:41
  40.8 32.5 %collective-permute-start.13 = (bf16[256,896]{1,0:T(8,128)(2,1)}, bf16[256,896]{1,0:T(8,128)(2,1)}, u32[]{:S(2)}, u32[]{:S(2)}) collective-permute-start(bf16[256,896]{1,0:T(8,128)(2,1)} %param.6), channel_id=1, source_target_pairs={{0,96},{32,0},{64,32},{96,64},{1,97},{33,1},{65,33},{97,65},{2,98}... | collective-permute-start | bytes 1376264 | tf_op jit(solution)/shard_map/ppermute | solution.py:41
  42.2 4.4 %collective-permute-start.2 = (f32[18432]{0:T(1024)S(1)}, f32[18432]{0:T(1024)S(1)}, u32[]{:S(2)}, u32[]{:S(2)}) collective-permute-start(f32[18432]{0:T(1024)S(1)} %fusion.31), channel_id=1, source_target_pairs={{0,2},{1,3},{2,0},{3,1},{4,6},{5,7},{6,4},{7,5},{8,10},{9,11},{10,... | collective-permute-start | bytes 221192 | tf_op jit(solution)/shard_map/ppermute | solution.py:58
  46.6 5.9 %collective-permute-start.3 = (f32[18432]{0:T(1024)S(1)}, f32[18432]{0:T(1024)S(1)}, u32[]{:S(2)}, u32[]{:S(2)}) collective-permute-start(f32[18432]{0:T(1024)S(1)} %add.132), channel_id=1, source_target_pairs={{0,4},{1,5},{2,6},{3,7},{4,0},{5,1},{6,2},{7,3},{8,12},{9,13},{10,... | collective-permute-start | bytes 221192 | tf_op jit(solution)/shard_map/ppermute | solution.py:58
  52.6 6.1 %collective-permute-start.4 = (f32[18432]{0:T(1024)S(1)}, f32[18432]{0:T(1024)S(1)}, u32[]{:S(2)}, u32[]{:S(2)}) collective-permute-start(f32[18432]{0:T(1024)S(1)} %add.133), channel_id=1, source_target_pairs={{0,8},{1,9},{2,10},{3,11},{4,12},{5,13},{6,14},{7,15},{8,0},{9,1},... | collective-permute-start | bytes 221192 | tf_op jit(solution)/shard_map/ppermute | solution.py:58
  58.7 6.5 %collective-permute-start.5 = (f32[18432]{0:T(1024)S(1)}, f32[18432]{0:T(1024)S(1)}, u32[]{:S(2)}, u32[]{:S(2)}) collective-permute-start(f32[18432]{0:T(1024)S(1)} %add.134), channel_id=1, source_target_pairs={{0,16},{1,17},{2,18},{3,19},{4,20},{5,21},{6,22},{7,23},{8,24},{9,... | collective-permute-start | bytes 221192 | tf_op jit(solution)/shard_map/ppermute | solution.py:58
  65.4 18.7 %collective-permute-start.14 = (f32[256,64]{1,0:T(8,128)S(1)}, f32[256,64]{1,0:T(8,128)}, u32[]{:S(2)}, u32[]{:S(2)}) collective-permute-start(f32[256,64]{1,0:T(8,128)S(1)} %slice.18), channel_id=1, source_target_pairs={{0,32},{32,64},{64,96},{96,0},{1,33},{33,65},{65,97},{97,1},{2,34}... | collective-permute-start | bytes 196616 | tf_op jit(solution)/shard_map/ppermute | solution.py:41
  66.9 20.2 %collective-permute-start.15 = (f32[256,64]{1,0:T(8,128)S(1)}, f32[256,64]{1,0:T(8,128)}, u32[]{:S(2)}, u32[]{:S(2)}) collective-permute-start(f32[256,64]{1,0:T(8,128)S(1)} %slice.18), channel_id=1, source_target_pairs={{0,64},{32,96},{64,0},{96,32},{1,65},{33,97},{65,1},{97,33},{2,66}... | collective-permute-start | bytes 196616 | tf_op jit(solution)/shard_map/ppermute | solution.py:41
  67.4 24.9 %collective-permute-start.16 = (f32[256,64]{1,0:T(8,128)S(1)}, f32[256,64]{1,0:T(8,128)S(1)}, u32[]{:S(2)}, u32[]{:S(2)}) collective-permute-start(f32[256,64]{1,0:T(8,128)S(1)} %slice.18), channel_id=1, source_target_pairs={{0,96},{32,0},{64,32},{96,64},{1,97},{33,1},{65,33},{97,65},{2,98}... | collective-permute-start | bytes 196616 | tf_op jit(solution)/shard_map/ppermute | solution.py:41
  71.3 0.8 copy-start.3
  84.0 20.5 %copy-start.5 = (f32[2048]{0:T(1024)S(1)}, f32[2048]{0:T(1024)}, u32[]{:S(2)}) copy-start(f32[2048]{0:T(1024)} %param.11) | copy-start | bytes 24580
  84.0 1.3 collective-permute-start.17
  85.3 3.7 %collective-permute-start.18 = (f32[2048]{0:T(1024)S(1)}, f32[2048]{0:T(1024)S(1)}, u32[]{:S(2)}, u32[]{:S(2)}) collective-permute-start(f32[2048]{0:T(1024)S(1)} %add.157), channel_id=1, source_target_pairs={{0,2},{1,3},{2,0},{3,1},{4,6},{5,7},{6,4},{7,5},{8,10},{9,11},{10,... | collective-permute-start | bytes 24584 | tf_op jit(solution)/shard_map/ppermute | solution.py:58
  88.9 5.2 %collective-permute-start.19 = (f32[2048]{0:T(1024)S(1)}, f32[2048]{0:T(1024)S(1)}, u32[]{:S(2)}, u32[]{:S(2)}) collective-permute-start(f32[2048]{0:T(1024)S(1)} %add.158), channel_id=1, source_target_pairs={{0,4},{1,5},{2,6},{3,7},{4,0},{5,1},{6,2},{7,3},{8,12},{9,13},{10,... | collective-permute-start | bytes 24584 | tf_op jit(solution)/shard_map/ppermute | solution.py:58
  92.4 12.7 %copy-start.1 = (bf16[256,8192]{0,1:T(8,128)(2,1)S(1)}, bf16[256,8192]{0,1:T(8,128)(2,1)}, u32[]{:S(2)}) copy-start(bf16[256,8192]{0,1:T(8,128)(2,1)} %all-gather.2.cloned.1.call-done) | copy-start | bytes 12582916
  94.1 3.7 %collective-permute-start.20 = (f32[2048]{0:T(1024)S(1)}, f32[2048]{0:T(1024)S(1)}, u32[]{:S(2)}, u32[]{:S(2)}) collective-permute-start(f32[2048]{0:T(1024)S(1)} %add.159), channel_id=1, source_target_pairs={{0,8},{1,9},{2,10},{3,11},{4,12},{5,13},{6,14},{7,15},{8,0},{9,1},... | collective-permute-start | bytes 24584 | tf_op jit(solution)/shard_map/ppermute | solution.py:58
  97.7 6.8 %collective-permute-start.21 = (f32[2048]{0:T(1024)S(1)}, f32[2048]{0:T(1024)S(1)}, u32[]{:S(2)}, u32[]{:S(2)}) collective-permute-start(f32[2048]{0:T(1024)S(1)} %add.160), channel_id=1, source_target_pairs={{0,16},{1,17},{2,18},{3,19},{4,20},{5,21},{6,22},{7,23},{8,24},{9,... | collective-permute-start | bytes 24584 | tf_op jit(solution)/shard_map/ppermute | solution.py:58
  112.6 29.6 %collective-permute-start.6 = (bf16[256,896]{0,1:T(8,128)(2,1)S(1)}, bf16[256,896]{0,1:T(8,128)(2,1)S(1)}, u32[]{:S(2)}, u32[]{:S(2)}) collective-permute-start(bf16[256,896]{0,1:T(8,128)(2,1)S(1)} %get-tuple-element.12), channel_id=1, source_target_pairs={{0,32},{32,64},{64,96},{96,0},{1,33},{33,65},{65,97},{97,1},{2,34}... | collective-permute-start | bytes 1376264 | tf_op jit(solution)/shard_map/ppermute | solution.py:50
  112.7 29.5 %collective-permute-start.7 = (bf16[256,896]{0,1:T(8,128)(2,1)S(1)}, bf16[256,896]{0,1:T(8,128)(2,1)S(1)}, u32[]{:S(2)}, u32[]{:S(2)}) collective-permute-start(bf16[256,896]{0,1:T(8,128)(2,1)S(1)} %get-tuple-element.14), channel_id=1, source_target_pairs={{0,64},{32,96},{64,0},{96,32},{1,65},{33,97},{65,1},{97,33},{2,66}... | collective-permute-start | bytes 1376264 | tf_op jit(solution)/shard_map/ppermute | solution.py:50
  114.2 28.1 %collective-permute-start.8 = (bf16[256,896]{0,1:T(8,128)(2,1)S(1)}, bf16[256,896]{0,1:T(8,128)(2,1)S(1)}, u32[]{:S(2)}, u32[]{:S(2)}) collective-permute-start(bf16[256,896]{0,1:T(8,128)(2,1)S(1)} %get-tuple-element.13), channel_id=1, source_target_pairs={{0,96},{32,0},{64,32},{96,64},{1,97},{33,1},{65,33},{97,65},{2,98}... | collective-permute-start | bytes 1376264 | tf_op jit(solution)/shard_map/ppermute | solution.py:50
  117.0 25.0 %collective-permute-start.9 = (f32[4,256,64]{1,2,0:T(8,128)S(1)}, f32[4,256,64]{1,2,0:T(8,128)S(1)}, u32[]{:S(2)}, u32[]{:S(2)}) collective-permute-start(f32[4,256,64]{1,2,0:T(8,128)S(1)} %fusion.9), channel_id=1, source_target_pairs={{0,32},{32,0},{64,96},{96,64},{1,33},{33,1},{65,97},{97,65},{2,34}... | collective-permute-start | bytes 786440 | tf_op jit(solution)/shard_map/ppermute | solution.py:58
  142.1 8.0 %collective-permute-start.10 = (f32[4,256,64]{1,2,0:T(8,128)S(1)}, f32[4,256,64]{1,2,0:T(8,128)S(1)}, u32[]{:S(2)}, u32[]{:S(2)}) collective-permute-start(f32[4,256,64]{1,2,0:T(8,128)S(1)} %add.153), channel_id=1, source_target_pairs={{0,64},{32,96},{64,0},{96,32},{1,65},{33,97},{65,1},{97,33},{2,66}... | collective-permute-start | bytes 786440 | tf_op jit(solution)/shard_map/ppermute | solution.py:58
Sparse Core Ops, SparseCore 0:
  10.8 59.0 all-gather.1
